TPU v7x, 128 devices: a whole 4x4x4 slice. The times are simulated.
128 devices in a mesh: dp: 8 (over x_hi, z), tensor: 16 (over y, x_lo, core).
Axes of the slice: x: 4 (x_hi: 2, x_lo: 2; x = x_hi * 2 + x_lo), y: 4, z: 4, core: 2. Of those that a mesh axis runs over, the one named last changes fastest.
Arguments:
- tokens: bfloat16 [16384, 2048], P(('dp', 'tensor')), parts along dimension 0, may hold values from -6 to 6
- segment_ids: int32 [16384], P('dp'), parts along dimension 0, may hold values from 0 to 3, never falling along the last dimension, each value on 1 to 1024 neighbouring positions
- attention_gain: float32 [2048], replicated, may hold values from 0.1 to 1.9
- query_weight: bfloat16 [2048, 2048], P(None, 'tensor'), may hold values from -1 to 1
- key_weight: bfloat16 [2048, 2048], P(None, 'tensor'), may hold values from -1 to 1
- value_weight: bfloat16 [2048, 2048], P(None, 'tensor'), may hold values from -0.125 to 0.125
- output_weight: bfloat16 [2048, 2048], P('tensor'), may hold values from -0.125 to 0.125
- ffn_gain: float32 [2048], replicated, may hold values from 0.1 to 1.9
- shared_gate: bfloat16 [2048, 2816], P(None, 'tensor'), may hold values from -0.125 to 0.125
- shared_up: bfloat16 [2048, 2816], P(None, 'tensor'), may hold values from -0.125 to 0.125
- shared_down: bfloat16 [2816, 2048], P('tensor'), may hold values from -0.109375 to 0.109375
- expert_gate: bfloat16 [16, 2048, 1408], P('tensor'), may hold values from -0.125 to 0.125
- expert_up: bfloat16 [16, 2048, 1408], P('tensor'), may hold values from -0.125 to 0.125
- expert_down: bfloat16 [16, 1408, 2048], P('tensor'), may hold values from -0.15625 to 0.15625
- expert_ids: int32 [16384, 6], P('dp'), parts along dimension 0, may hold values from 0 to 15, all different within a row; in each aligned block of 128 rows (0 to 127, 128 to 255, ...) at most 64 rows name the same one
- gate_weights: float32 [16384, 6], P('dp'), parts along dimension 0, may hold values from 0.05 to 0.35
- page_table: int32 [128], P('dp'), parts along dimension 0, may hold values from 0 to 15, each once
Outputs:
- layer_out: bfloat16 [16384, 2048], P(('dp', 'tensor')), parts along dimension 0
- kv_pages: bfloat16 [2, 128, 128, 2048], P(None, 'dp', None, 'tensor'), parts along dimension 1
There are 8 independent parts, one for each index of `dp`. A program takes and returns all parts, laid end to end along the dimension named above; an argument that names none is the same for every part. Nothing has to cross between parts.
Inputs may be any that keep to these rules, and one draw needn't show every extreme that they name: `segment_ids`: ids never fall along the stream; each of the 4 prompts holds 1 to 1024 tokens and one holds exactly 1024. `expert_ids`: each row names 6 different experts; within each aligned block of 128 rows (the tokens of one index of tensor) no expert is named by more than 64 rows, a bound that some block reaches. `page_table`: each cache page is named once.
All inputs are finite; a program needn't handle non-finite values.
Results may differ from a plain program's by a relative error of at most 0.02.
The roundings to bfloat16 on the way count: a program that leaves them out, or rounds other values in their place, can miss the bound.
Values may be sent and summed in bfloat16 or wider, within the bound.
No kernel may reach another device: no remote copies, remote signals or barrier semaphores. Data moves between devices by JAX's collectives and lax.ppermute only.
A program may use at most 128 MiB of HBM per device.

v0:
```python
import jax
import jax.numpy as jnp
from jax import lax
from jax.sharding import PartitionSpec as P

HD = 128
TOP = 6
PAGE = 128


def rms_scale(hidden, gain):
    widened = hidden.astype(jnp.float32)
    inverse = lax.rsqrt(jnp.mean(widened * widened, axis=-1, keepdims=True) + 1e-06)
    return (widened * inverse * gain).astype(jnp.bfloat16)


def attend(projected, segment_ids, head_count):
    total_tokens = projected.shape[0]
    inner = head_count * HD
    queries = projected[:, :inner].reshape(total_tokens, head_count, HD)
    keys = projected[:, inner : 2 * inner].reshape(total_tokens, head_count, HD)
    values = projected[:, 2 * inner :].reshape(total_tokens, head_count, HD)
    scale = HD ** (-0.5)
    positions = jnp.arange(total_tokens, dtype=jnp.int32)
    span = min(512, total_tokens)

    def one_block(start):
        query_rows = lax.dynamic_slice_in_dim(queries, start, span, 0)
        query_segments = lax.dynamic_slice_in_dim(segment_ids, start, span, 0)
        query_positions = start + jnp.arange(span, dtype=jnp.int32)
        scores = (
            jnp.einsum("qhd,khd->hqk", query_rows, keys, preferred_element_type=jnp.float32) * scale
        )
        allowed = (query_segments[:, None] == segment_ids[None, :]) & (
            positions[None, :] <= query_positions[:, None]
        )
        scores = jnp.where(allowed[None], scores, -jnp.inf)
        highest = jnp.max(scores, axis=-1, keepdims=True)
        weights = jnp.exp(scores - highest)
        probs = (weights / jnp.sum(weights, axis=-1, keepdims=True)).astype(jnp.bfloat16)
        context = jnp.einsum("hqk,khd->qhd", probs, values, preferred_element_type=jnp.float32)
        return context.astype(jnp.bfloat16)

    starts = jnp.arange(total_tokens // span, dtype=jnp.int32) * span
    context = lax.map(one_block, starts).reshape(total_tokens, inner)
    return (context, keys.reshape(total_tokens, inner), values.reshape(total_tokens, inner))


def expert_apply(picked, gate_w, up_w, down_w):
    gate_part = jnp.dot(picked, gate_w, preferred_element_type=jnp.float32)
    upward = jnp.dot(picked, up_w, preferred_element_type=jnp.float32)
    hidden = (jax.nn.silu(gate_part) * upward).astype(jnp.bfloat16)
    return jnp.dot(hidden, down_w, preferred_element_type=jnp.float32).astype(jnp.bfloat16)


def ring_reduce_scatter(partial, groups):
    ring = groups // 4
    rows = partial.shape[0] // groups
    width = partial.shape[1]
    me = lax.axis_index("tensor")
    y = me // 4
    side = me // 2 % 2
    core = me % 2
    blocks = partial.reshape(ring, 2, 2, rows, width)
    core_pairs = [(t, t ^ 1) for t in range(groups)]
    keep = lax.dynamic_index_in_dim(blocks, core, axis=2, keepdims=False)
    give = lax.dynamic_index_in_dim(blocks, 1 - core, axis=2, keepdims=False)
    got = lax.ppermute(give, "tensor", core_pairs)
    summed = keep.astype(jnp.float32) + got.astype(jnp.float32)
    half = width // 2
    forward_part = summed[..., :half]
    backward_part = summed[..., half:]
    forward_pairs = [(t, (t // 4 + 1) % ring * 4 + t % 4) for t in range(groups)]
    backward_pairs = [(t, (t // 4 + ring - 1) % ring * 4 + t % 4) for t in range(groups)]
    carry_f = lax.dynamic_index_in_dim(forward_part, (y + ring - 1) % ring, 0, False)
    carry_b = lax.dynamic_index_in_dim(backward_part, (y + 1) % ring, 0, False)
    carry_f = carry_f.astype(jnp.bfloat16)
    carry_b = carry_b.astype(jnp.bfloat16)
    for step in range(ring - 1):
        recv_f = lax.ppermute(carry_f, "tensor", forward_pairs)
        recv_b = lax.ppermute(carry_b, "tensor", backward_pairs)
        index_f = (y + 2 * ring - step - 2) % ring
        index_b = (y + step + 2) % ring
        acc_f = recv_f.astype(jnp.float32) + lax.dynamic_index_in_dim(
            forward_part, index_f, 0, False
        )
        acc_b = recv_b.astype(jnp.float32) + lax.dynamic_index_in_dim(
            backward_part, index_b, 0, False
        )
        carry_f = acc_f.astype(jnp.bfloat16)
        carry_b = acc_b.astype(jnp.bfloat16)
    mine = jnp.concatenate([acc_f, acc_b], axis=-1)
    side_pairs = [(t, t ^ 2) for t in range(groups)]
    keep_side = lax.dynamic_index_in_dim(mine, side, 0, False)
    give_side = lax.dynamic_index_in_dim(mine, 1 - side, 0, False).astype(jnp.bfloat16)
    got_side = lax.ppermute(give_side, "tensor", side_pairs)
    return keep_side + got_side.astype(jnp.float32)


def shards(
    tokens,
    segment_ids,
    attention_gain,
    query_weight,
    key_weight,
    value_weight,
    output_weight,
    ffn_gain,
    shared_gate,
    shared_up,
    shared_down,
    expert_gate,
    expert_up,
    expert_down,
    expert_ids,
    gate_weights,
    page_table,
):
    tok_dev = tokens.shape[0]
    groups = lax.axis_size("tensor")
    position = lax.axis_index("tensor")
    inner = query_weight.shape[1]
    head_count = inner // HD
    model_width = tokens.shape[1]
    projection = jnp.concatenate([query_weight, key_weight, value_weight], axis=1)
    normed_all = lax.all_gather(rms_scale(tokens, attention_gain), "tensor", axis=0, tiled=True)
    out_weight_all = lax.all_gather(output_weight, "tensor", axis=0, tiled=True)
    projected = lax.map(
        lambda rows: jnp.dot(rows, projection, preferred_element_type=jnp.float32).astype(
            jnp.bfloat16
        ),
        normed_all.reshape(4, -1, normed_all.shape[1]),
    ).reshape(normed_all.shape[0], -1)
    context, keys, values = attend(projected, segment_ids, head_count)
    cache = jnp.stack([keys, values]).reshape(2, -1, PAGE, inner)
    kv_pages = jnp.zeros_like(cache).at[:, page_table].set(cache)
    received = lax.all_to_all(
        context.reshape(groups, tok_dev, inner), "tensor", split_axis=0, concat_axis=0, tiled=True
    )
    context_rows = received.transpose(1, 0, 2).reshape(tok_dev, groups * inner)
    attention = jnp.dot(context_rows, out_weight_all, preferred_element_type=jnp.float32)
    residual = (tokens.astype(jnp.float32) + attention).astype(jnp.bfloat16)
    normed_ffn = rms_scale(residual, ffn_gain)
    pieces = 2
    piece_width = model_width // pieces
    normed_stream = lax.all_gather(normed_ffn, "tensor", axis=0, tiled=True)
    local_experts = expert_gate.shape[0]
    expert_count = local_experts * groups
    capacity = tok_dev * TOP // expert_count + tok_dev // 8
    id_blocks = expert_ids.reshape(groups, tok_dev, -1)
    gate_blocks = gate_weights.reshape(groups, tok_dev, -1)
    slots = jnp.arange(capacity, dtype=jnp.int32)
    onehots = []
    weights = []
    for local in range(local_experts):
        expert = position * local_experts + local
        chosen = id_blocks == expert
        hits = jnp.sum(chosen.astype(jnp.int32), axis=2)
        weights.append(jnp.sum(jnp.where(chosen, gate_blocks, 0.0), axis=2))
        rank = jnp.cumsum(hits, axis=1) - hits
        onehots.append(
            ((hits[:, None, :] > 0) & (rank[:, None, :] == slots[None, :, None])).astype(
                jnp.bfloat16
            )
        )
    shared_columns = jnp.concatenate([shared_gate, shared_up], axis=1)
    shared_width = shared_gate.shape[1]
    joined = jnp.dot(normed_stream, shared_columns, preferred_element_type=jnp.float32)
    token_blocks = normed_stream.reshape(groups, tok_dev, model_width)
    expert_gate_parts = []
    expert_up_parts = []
    for local in range(local_experts):
        picked = (
            jnp.einsum(
                "bst,btd->bsd", onehots[local], token_blocks, preferred_element_type=jnp.float32
            )
            .astype(jnp.bfloat16)
            .reshape(-1, model_width)
        )
        expert_gate_parts.append(
            jnp.dot(picked, expert_gate[local], preferred_element_type=jnp.float32)
        )
        expert_up_parts.append(
            jnp.dot(picked, expert_up[local], preferred_element_type=jnp.float32)
        )
    hidden_all = (jax.nn.silu(joined[:, :shared_width]) * joined[:, shared_width:]).astype(
        jnp.bfloat16
    )
    expert_hidden = [
        (jax.nn.silu(expert_gate_parts[local]) * expert_up_parts[local]).astype(jnp.bfloat16)
        for local in range(local_experts)
    ]
    outs = []
    for k in range(pieces):
        columns = slice(k * piece_width, (k + 1) * piece_width)
        term = jnp.dot(hidden_all, shared_down[:, columns], preferred_element_type=jnp.float32)
        for local in range(local_experts):
            rows = jnp.dot(
                expert_hidden[local],
                expert_down[local][:, columns],
                preferred_element_type=jnp.float32,
            ).astype(jnp.bfloat16)
            back = jnp.einsum(
                "bst,bsd->btd",
                onehots[local],
                rows.reshape(groups, capacity, piece_width),
                preferred_element_type=jnp.float32,
            ).astype(jnp.bfloat16)
            term = term + weights[local].reshape(-1, 1) * back.reshape(-1, piece_width).astype(
                jnp.float32
            )
        outs.append(ring_reduce_scatter(term.astype(jnp.bfloat16), groups))
    ffn_out = jnp.concatenate(outs, axis=1)
    layer_out = (residual.astype(jnp.float32) + ffn_out).astype(jnp.bfloat16)
    return (layer_out, kv_pages)


def solution(mesh):
    placed = (
        P(("dp", "tensor"), None),
        P("dp"),
        P(),
        P(None, "tensor"),
        P(None, "tensor"),
        P(None, "tensor"),
        P("tensor", None),
        P(),
        P(None, "tensor"),
        P(None, "tensor"),
        P("tensor", None),
        P("tensor", None, None),
        P("tensor", None, None),
        P("tensor", None, None),
        P("dp", None),
        P("dp", None),
        P("dp"),
    )
    return jax.shard_map(
        shards,
        mesh=mesh,
        in_specs=placed,
        out_specs=(P(("dp", "tensor"), None), P(None, "dp", None, "tensor")),
        check_vma=False,
    )
```

profile of v0, /device:TPU:0, one launch (start us, length us, event | category | flops | bytes accessed | tf_op | source)
XLA Modules:
  0.0 287.7 jit_solution(262670037977427516)
XLA Ops:
  8.4 2.0 fusion.55
  12.9 52.3 %all-gather.4.cloned.1.call-done = bf16[2048,2048]{1,0:T(8,128)(2,1)} async-done(((bf16[128,2048]{1,0:T(8,128)(2,1)}), bf16[2048,2048]{1,0:T(8,128)(2,1)}) %all-gather.4.cloned.1.call-update) | async-done | bytes 8388624 | tf_op jit(solution)/shard_map/all_gather | solution.py:126
  65.2 14.6 %while.21 = (s32[]{:T(128)}, bf16[4,512,384]{2,1,0:T(8,128)(2,1)}, bf16[4,512,2048]{2,1,0:T(8,128)(2,1)}, bf16[2048,384]{1,0:T(8,128)(2,1)S(1)}, s32[]{:T(128)}) while((s32[]{:T(128)}, bf16[4,512,384]{2,1,0:T(8,128)(2,1)}, bf16[4,512,2048]{2,1,0:T(8,128)(2,1)}, bf16[2048,384]{1,0:T(8,128)(2,1)S(1)}, s32[]{:T(128)}) %tuple.62), condition=%wide.region_2.3_spmd, body=%wide.region_1.2_spmd.sunk | while | flops 805502976 | bytes 4064325 | solution.py:128
  65.2 3.6 %fusion.120 = bf16[4,512,384]{2,1,0:T(8,128)(2,1)} fusion(bf16[4,512,384]{2,1,0:T(8,128)(2,1)} %get-tuple-element.199, s32[]{:T(128)S(6)} %copy.34, bf16[2048,384]{1,0:T(8,128)(2,1)S(1)} %get-tuple-element.206, bf16[4,512,2048]{2,1,0:T(8,128)(2,1)} %get-tuple-element.205), kind=kOutput, calls=%fused_computation.7.clone.1 | convolution fusion | flops 805502976 | bytes 4064256 | tf_op jit(solution)/shard_map/while/body/eval_jaxpr/dot_general | solution.py:129
  68.8 3.6 %fusion.120 = bf16[4,512,384]{2,1,0:T(8,128)(2,1)} fusion(bf16[4,512,384]{2,1,0:T(8,128)(2,1)} %get-tuple-element.199, s32[]{:T(128)S(6)} %copy.34, bf16[2048,384]{1,0:T(8,128)(2,1)S(1)} %get-tuple-element.206, bf16[4,512,2048]{2,1,0:T(8,128)(2,1)} %get-tuple-element.205), kind=kOutput, calls=%fused_computation.7.clone.1 | convolution fusion | flops 805502976 | bytes 4064256 | tf_op jit(solution)/shard_map/while/body/eval_jaxpr/dot_general | solution.py:129
  72.4 3.6 %fusion.120 = bf16[4,512,384]{2,1,0:T(8,128)(2,1)} fusion(bf16[4,512,384]{2,1,0:T(8,128)(2,1)} %get-tuple-element.199, s32[]{:T(128)S(6)} %copy.34, bf16[2048,384]{1,0:T(8,128)(2,1)S(1)} %get-tuple-element.206, bf16[4,512,2048]{2,1,0:T(8,128)(2,1)} %get-tuple-element.205), kind=kOutput, calls=%fused_computation.7.clone.1 | convolution fusion | flops 805502976 | bytes 4064256 | tf_op jit(solution)/shard_map/while/body/eval_jaxpr/dot_general | solution.py:129
  76.0 3.8 %fusion.120 = bf16[4,512,384]{2,1,0:T(8,128)(2,1)} fusion(bf16[4,512,384]{2,1,0:T(8,128)(2,1)} %get-tuple-element.199, s32[]{:T(128)S(6)} %copy.34, bf16[2048,384]{1,0:T(8,128)(2,1)S(1)} %get-tuple-element.206, bf16[4,512,2048]{2,1,0:T(8,128)(2,1)} %get-tuple-element.205), kind=kOutput, calls=%fused_computation.7.clone.1 | convolution fusion | flops 805502976 | bytes 4064256 | tf_op jit(solution)/shard_map/while/body/eval_jaxpr/dot_general | solution.py:129
  79.8 2.6 fusion.97
  82.5 23.1 %while.22 = (s32[]{:T(128)}, bf16[4,512,1,128]{3,1,2,0:T(8,128)(2,1)S(1)}, s32[4]{0:T(128)S(1)}, s32[2048]{0:T(1024)S(1)}, bf16[2048,1,128]{2,0,1:T(8,128)(2,1)S...) while((s32[]{:T(128)}, ...), condition=%wide.region_6.7_spmd.clone, body=%wide.region_3.6_spmd.clone.sunk | while | flops 548470272 | bytes 13922475 | solution.py:45
  105.6 20.5 %all_to_all.5 = bf16[16,128,128]{2,1,0:T(8,128)(2,1)S(1)} all-to-all(bf16[16,128,128]{2,1,0:T(8,128)(2,1)S(1)} %bitcast.200), channel_id=1, replica_groups=mesh['dp'=8,'tensor'=16] {'tensor'}, dimensions={0} | all-to-all | bytes 1048576 | tf_op jit(solution)/shard_map/all_to_all | solution.py:137
  126.4 4.8 %multiply_reduce_fusion = (f32[128]{0:T(128)S(1)}, f32[128,2048]{1,0:T(8,128)S(1)}) fusion(bf16[128,2048]{0,1:T(8,128)(2,1)S(1)} %bitcast.193, bf16[2048,2048]{1,0:T(8,128)(2,1)} %all-gather.6.cloned.1.call-done, bf16[128,2048]{1,0:T(8,128)(2,1)S(1)} %copy-done), kind=kOutput, calls=%fused_computation.76 | convolution fusion | flops 1075314560 | bytes 10486272 | tf_op jit(solution)/shard_map/dot_general | solution.py:141
  132.7 52.0 %all-gather.8.cloned.1.call-done = bf16[2048,2048]{1,0:T(8,128)(2,1)} async-done(((bf16[128,2048]{1,0:T(8,128)(2,1)}), bf16[2048,2048]{1,0:T(8,128)(2,1)}) %all-gather.8.cloned.1.call-update) | async-done | bytes 8388624 | tf_op jit(solution)/shard_map/all_gather | solution.py:146
  184.7 4.8 %convolution_convert_fusion = bf16[16,64,2048]{2,1,0:T(8,128)(2,1)S(1)} fusion(bf16[16,128,2048]{2,1,0:T(8,128)(2,1)} %bitcast.182, s32[16,128]{1,0:T(8,128)S(1)} %bitcast_subtract_fusion, pred[16,128]{1,0:T(8,128)(4,1)S(1)} %broadcast_compare_fusion.1), kind=kOutput, calls=%fused_computation.38 | convolution fusion | flops 539230208 | bytes 12593152 | tf_op jit(solution)/shard_map/bst,btd->bsd/dot_general | solution.py:174
  189.5 9.4 %fusion.32 = f32[1024,1408]{1,0:T(8,128)S(1)} fusion(bf16[1024,2048]{1,0:T(8,128)(2,1)S(1)} %bitcast.185, bf16[1,2048,1408]{2,1,0:T(8,128)(2,1)} %param.32), kind=kOutput, calls=%fused_computation.33 | convolution fusion | flops 5905580032 | bytes 15728640 | tf_op jit(solution)/shard_map/dot_general | solution.py:181
  198.9 7.0 %multiply_convert_fusion = bf16[1024,1408]{1,0:T(8,128)(2,1)S(1)} fusion(f32[1024,1408]{1,0:T(8,128)S(1)} %fusion.32, bf16[1024,2048]{1,0:T(8,128)(2,1)S(1)} %bitcast.186, bf16[1,2048,1408]{2,1,0:T(8,128)(2,1)S(1)} %bitcast.204), kind=kOutput, calls=%fused_computation.35 | convolution fusion | flops 5914230784 | bytes 18612224 | tf_op jit(solution)/shard_map/dot_general | solution.py:184
  206.0 3.6 %fusion.45 = bf16[1024,1024]{1,0:T(8,128)(2,1)S(1)} fusion(bf16[1024,1408]{1,0:T(8,128)(2,1)S(1)} %multiply_convert_fusion, bf16[1408,2048]{1,0:T(8,128)(2,1)S(1)} %bitcast.207), kind=kOutput, calls=%fused_computation.51 | convolution fusion | flops 2953838592 | bytes 7864320 | tf_op jit(solution)/shard_map/dot_general | solution.py:198
  209.7 3.9 %fusion.42 = bf16[1024,1024]{1,0:T(8,128)(2,1)S(1)} fusion(bf16[1024,1408]{1,0:T(8,128)(2,1)S(1)} %multiply_convert_fusion, bf16[1408,2048]{1,0:T(8,128)(2,1)S(1)} %bitcast.208), kind=kOutput, calls=%fused_computation.50 | convolution fusion | flops 2953838592 | bytes 7864320 | tf_op jit(solution)/shard_map/dot_general | solution.py:198
  213.6 3.2 %fusion.49 = f32[2048,352]{0,1:T(8,128)S(1)} fusion(bf16[2048,2048]{1,0:T(8,128)(2,1)S(1)} %bitcast.184, bf16[2048,176]{0,1:T(8,128)(2,1)S(1)} %copy-done.10, bf16[2048,176]{0,1:T(8,128)(2,1)S(1)} %copy-done.11), kind=kOutput, calls=%fused_computation.57 | convolution fusion | flops 2955673600 | bytes 12713984 | tf_op jit(solution)/shard_map/dot_general | solution.py:168
  225.3 2.0 copy-done.1
  227.8 3.2 %convert_add_fusion = f32[4,2,128,1024]{3,2,1,0:T(8,128)S(1)} fusion(bf16[4,2,128,1024]{3,2,1,0:T(8,128)(2,1)} %collective-permute-done.8, bf16[4,2,2,128,1024]{4,3,2,1,0:T(8,128)(2,1)} %bitcast.192, s32[]{:T(128)S(6)} %select_n.134), kind=kLoop, calls=%fused_computation.36 | loop fusion | flops 3145728 | bytes 8388612 | tf_op jit(solution)/shard_map/add | solution.py:69
  235.1 2.5 convert_add_fusion.1
  238.9 3.0 %collective-permute-start.4 = (bf16[2,128,512]{2,1,0:T(8,128)(2,1)S(1)}, bf16[2,128,512]{2,1,0:T(8,128)(2,1)S(1)}, u32[]{:S(2)}, u32[]{:S(2)}) collective-permute-start(bf16[2,128,512]{2,1,0:T(8,128)(2,1)S(1)} %fusion.82), channel_id=1, source_target_pairs={{0,12},{1,13},{2,14},{3,15},{4,0},{5,1},{6,2},{7,3},{8,4},{9,5},{1... | collective-permute-start | bytes 786440 | tf_op jit(solution)/shard_map/ppermute | solution.py:81
  242.3 3.1 %collective-permute-start.13 = (bf16[2,128,512]{2,1,0:T(8,128)(2,1)S(1)}, bf16[2,128,512]{2,1,0:T(8,128)(2,1)S(1)}, u32[]{:S(2)}, u32[]{:S(2)}) collective-permute-start(bf16[2,128,512]{2,1,0:T(8,128)(2,1)S(1)} %fusion.68), channel_id=1, source_target_pairs={{0,12},{1,13},{2,14},{3,15},{4,0},{5,1},{6,2},{7,3},{8,4},{9,5},{1... | collective-permute-start | bytes 786440 | tf_op jit(solution)/shard_map/ppermute | solution.py:81
  245.4 3.7 %collective-permute-done.1 = bf16[2,128,512]{2,1,0:T(8,128)(2,1)S(1)} collective-permute-done((bf16[2,128,512]{2,1,0:T(8,128)(2,1)S(1)}, bf16[2,128,512]{2,1,0:T(8,128)(2,1)S(1)}, u32[]{:S(2)}, u32[]{:S(2)}) %collective-permute-start.1) | collective-permute-done | bytes 262176 | tf_op jit(solution)/shard_map/ppermute | solution.py:80
  249.3 3.3 %collective-permute-start.5 = (bf16[2,128,512]{2,1,0:T(8,128)(2,1)S(1)}, bf16[2,128,512]{2,1,0:T(8,128)(2,1)S(1)}, u32[]{:S(2)}, u32[]{:S(2)}) collective-permute-start(bf16[2,128,512]{2,1,0:T(8,128)(2,1)S(1)} %fusion.72), channel_id=1, source_target_pairs={{0,12},{1,13},{2,14},{3,15},{4,0},{5,1},{6,2},{7,3},{8,4},{9,5},{1... | collective-permute-start | bytes 786440 | tf_op jit(solution)/shard_map/ppermute | solution.py:81
  252.6 2.1 collective-permute-done.10
  254.9 3.3 %collective-permute-start.14 = (bf16[2,128,512]{2,1,0:T(8,128)(2,1)S(1)}, bf16[2,128,512]{2,1,0:T(8,128)(2,1)S(1)}, u32[]{:S(2)}, u32[]{:S(2)}) collective-permute-start(bf16[2,128,512]{2,1,0:T(8,128)(2,1)S(1)} %fusion.67), channel_id=1, source_target_pairs={{0,12},{1,13},{2,14},{3,15},{4,0},{5,1},{6,2},{7,3},{8,4},{9,5},{1... | collective-permute-start | bytes 786440 | tf_op jit(solution)/shard_map/ppermute | solution.py:81
  258.2 2.1 collective-permute-done.2
  260.6 3.3 %collective-permute-start.6 = (bf16[2,128,512]{2,1,0:T(8,128)(2,1)S(1)}, bf16[2,128,512]{2,1,0:T(8,128)(2,1)S(1)}, u32[]{:S(2)}, u32[]{:S(2)}) collective-permute-start(bf16[2,128,512]{2,1,0:T(8,128)(2,1)S(1)} %fusion.71), channel_id=1, source_target_pairs={{0,12},{1,13},{2,14},{3,15},{4,0},{5,1},{6,2},{7,3},{8,4},{9,5},{1... | collective-permute-start | bytes 786440 | tf_op jit(solution)/shard_map/ppermute | solution.py:81
  263.9 2.1 collective-permute-done.11
  267.6 2.6 collective-permute-done.3
  274.8 3.4 %scatter_fusion = bf16[2,16,128,128]{3,2,1,0:T(8,128)(2,1)} fusion(bf16[2,16,128,128]{3,2,1,0:T(8,128)(2,1)} %broadcast_in_dim.45, s32[16]{0:T(128)S(1)} %compare_select_fusion, bf16[16,2,128,128]{3,2,1,0:T(8,128)(2,1)} %maximum_bitcast_fusion), kind=kCustom, calls=%fused_computation | custom fusion | bytes 3145792 | tf_op jit(solution)/shard_map/scatter | solution.py:136
  (142 shorter events, 46.4 us)
Async XLA Ops:
  7.2 58.1 %all-gather.4.cloned.1.call-start = ((), (), s32[]{:S(2)}) async-start(), calls=%async_computation.1 | async-start | bytes 8912896 | tf_op jit(solution)/shard_map/all_gather | solution.py:126
  10.5 115.9 %all-gather.6.cloned.1.call-start = ((), (), s32[]{:S(2)}) async-start(), calls=%async_computation.2 | async-start | bytes 8912896 | tf_op jit(solution)/shard_map/all_gather | solution.py:127
  11.3 173.4 %all-gather.8.cloned.1.call-start = ((), (), s32[]{:S(2)}) async-start(), calls=%async_computation.3 | async-start | bytes 8912896 | tf_op jit(solution)/shard_map/all_gather | solution.py:146
  82.5 43.9 %copy-start = (bf16[128,2048]{1,0:T(8,128)(2,1)S(1)}, bf16[128,2048]{1,0:T(8,128)(2,1)}, u32[]{:S(2)}) copy-start(bf16[128,2048]{1,0:T(8,128)(2,1)} %param.21) | copy-start | bytes 1572868
  126.4 4.8 %copy-start.9 = (f32[2048]{0:T(1024)S(1)}, f32[2048]{0:T(1024)}, u32[]{:S(2)}) copy-start(f32[2048]{0:T(1024)} %param.28) | copy-start | bytes 24580
  126.4 5.9 %copy-start.6 = (f32[2048,6]{0,1:T(8,128)S(1)}, f32[2048,6]{0,1:T(8,128)}, u32[]{:S(2)}) copy-start(f32[2048,6]{0,1:T(8,128)} %param.36) | copy-start | bytes 147460
  126.4 5.9 %copy-start.7 = (s32[2048,6]{0,1:T(8,128)S(1)}, s32[2048,6]{0,1:T(8,128)}, u32[]{:S(2)}) copy-start(s32[2048,6]{0,1:T(8,128)} %param.35) | copy-start | bytes 147460
  184.7 14.2 %slice-start.2 = ((s8[5767168]{0:T(1024)(128)(4,1)}), s8[4194304]{0:T(1024)(128)(4,1)S(1)}, s32[]{:S(2)}) async-start(s8[5767168]{0:T(1024)(128)(4,1)} %bitcast.203), calls=%async_computation.6 | async-start | bytes 8388608
  189.5 9.4 %slice-start.3 = ((s8[5767168]{0:T(1024)(128)(4,1)}), s8[1572864]{0:T(1024)(128)(4,1)S(1)}, s32[]{:S(2)}) async-start(s8[5767168]{0:T(1024)(128)(4,1)} %bitcast.203), calls=%async_computation.7 | async-start | bytes 3145728
  189.5 16.5 %slice-start.4 = ((s8[5767168]{0:T(1024)(128)(4,1)}), s8[4194304]{0:T(1024)(128)(4,1)S(1)}, s32[]{:S(2)}) async-start(s8[5767168]{0:T(1024)(128)(4,1)} %bitcast.205), calls=%async_computation.8 | async-start | bytes 8388608
  198.9 7.1 %slice-start.5 = ((s8[5767168]{0:T(1024)(128)(4,1)}), s8[1572864]{0:T(1024)(128)(4,1)S(1)}, s32[]{:S(2)}) async-start(s8[5767168]{0:T(1024)(128)(4,1)} %bitcast.205), calls=%async_computation.9 | async-start | bytes 3145728
  206.0 7.5 %slice-start = ((s8[8388608]{0:T(1024)(128)(4,1)}), s8[4194304]{0:T(1024)(128)(4,1)S(1)}, s32[]{:S(2)}) async-start(s8[8388608]{0:T(1024)(128)(4,1)} %bitcast.183), calls=%async_computation.4 | async-start | bytes 8388608
  209.6 3.9 %slice-start.1 = ((s8[8388608]{0:T(1024)(128)(4,1)}), s8[4194304]{0:T(1024)(128)(4,1)S(1)}, s32[]{:S(2)}) async-start(s8[8388608]{0:T(1024)(128)(4,1)} %bitcast.183), calls=%async_computation.5 | async-start | bytes 8388608
  222.0 5.8 %collective-permute-start.8 = (bf16[4,2,128,1024]{3,2,1,0:T(8,128)(2,1)}, bf16[4,2,128,1024]{3,2,1,0:T(8,128)(2,1)}, u32[]{:S(2)}, u32[]{:S(2)}) collective-permute-start(bf16[4,2,128,1024]{3,2,1,0:T(8,128)(2,1)} %dynamic-slice_bitcast_fusion), channel_id=1, source_target_pairs={{0,1},{1,0},{2,3},{3,2},{4,5},{5,4},{6,7},{7,6},{8,9},{9,8},{10,11... | collective-permute-start | bytes 6291464 | tf_op jit(solution)/shard_map/ppermute | solution.py:68
  227.4 7.6 %collective-permute-start = (bf16[4,2,128,1024]{3,2,1,0:T(8,128)(2,1)S(1)}, bf16[4,2,128,1024]{3,2,1,0:T(8,128)(2,1)}, u32[]{:S(2)}, u32[]{:S(2)}) collective-permute-start(bf16[4,2,128,1024]{3,2,1,0:T(8,128)(2,1)S(1)} %dynamic-slice_bitcast_fusion.1), channel_id=1, source_target_pairs={{0,1},{1,0},{2,3},{3,2},{4,5},{5,4},{6,7},{7,6},{8,9},{9,8},{10,11... | collective-permute-start | bytes 6291464 | tf_op jit(solution)/shard_map/ppermute | solution.py:68
  231.0 4.1 %copy-start.2 = (bf16[2048,1024]{1,0:T(8,128)(2,1)S(1)}, bf16[2048,1024]{1,0:T(8,128)(2,1)}, u32[]{:S(2)}) copy-start(bf16[2048,1024]{1,0:T(8,128)(2,1)} %copy-done.1) | copy-start | bytes 12582916
  231.7 10.2 %collective-permute-start.9 = (bf16[2,128,512]{2,1,0:T(8,128)(2,1)S(1)}, bf16[2,128,512]{2,1,0:T(8,128)(2,1)S(1)}, u32[]{:S(2)}, u32[]{:S(2)}) collective-permute-start(bf16[2,128,512]{2,1,0:T(8,128)(2,1)S(1)} %fusion.83), channel_id=1, source_target_pairs={{0,4},{1,5},{2,6},{3,7},{4,8},{5,9},{6,10},{7,11},{8,12},{9,13},{1... | collective-permute-start | bytes 786440 | tf_op jit(solution)/shard_map/ppermute | solution.py:80
  233.2 9.0 %collective-permute-start.12 = (bf16[2,128,512]{2,1,0:T(8,128)(2,1)S(1)}, bf16[2,128,512]{2,1,0:T(8,128)(2,1)S(1)}, u32[]{:S(2)}, u32[]{:S(2)}) collective-permute-start(bf16[2,128,512]{2,1,0:T(8,128)(2,1)S(1)} %fusion.84), channel_id=1, source_target_pairs={{0,12},{1,13},{2,14},{3,15},{4,0},{5,1},{6,2},{7,3},{8,4},{9,5},{1... | collective-permute-start | bytes 786440 | tf_op jit(solution)/shard_map/ppermute | solution.py:81
  238.3 10.8 %collective-permute-start.1 = (bf16[2,128,512]{2,1,0:T(8,128)(2,1)S(1)}, bf16[2,128,512]{2,1,0:T(8,128)(2,1)S(1)}, u32[]{:S(2)}, u32[]{:S(2)}) collective-permute-start(bf16[2,128,512]{2,1,0:T(8,128)(2,1)S(1)} %fusion.81), channel_id=1, source_target_pairs={{0,4},{1,5},{2,6},{3,7},{4,8},{5,9},{6,10},{7,11},{8,12},{9,13},{1... | collective-permute-start | bytes 786440 | tf_op jit(solution)/shard_map/ppermute | solution.py:80
  238.9 10.3 %collective-permute-start.4 = (bf16[2,128,512]{2,1,0:T(8,128)(2,1)S(1)}, bf16[2,128,512]{2,1,0:T(8,128)(2,1)S(1)}, u32[]{:S(2)}, u32[]{:S(2)}) collective-permute-start(bf16[2,128,512]{2,1,0:T(8,128)(2,1)S(1)} %fusion.82), channel_id=1, source_target_pairs={{0,12},{1,13},{2,14},{3,15},{4,0},{5,1},{6,2},{7,3},{8,4},{9,5},{1... | collective-permute-start | bytes 786440 | tf_op jit(solution)/shard_map/ppermute | solution.py:81
  242.0 12.7 %collective-permute-start.10 = (bf16[2,128,512]{2,1,0:T(8,128)(2,1)S(1)}, bf16[2,128,512]{2,1,0:T(8,128)(2,1)S(1)}, u32[]{:S(2)}, u32[]{:S(2)}) collective-permute-start(bf16[2,128,512]{2,1,0:T(8,128)(2,1)S(1)} %fusion.70), channel_id=1, source_target_pairs={{0,4},{1,5},{2,6},{3,7},{4,8},{5,9},{6,10},{7,11},{8,12},{9,13},{1... | collective-permute-start | bytes 786440 | tf_op jit(solution)/shard_map/ppermute | solution.py:80
  242.3 12.5 %collective-permute-start.13 = (bf16[2,128,512]{2,1,0:T(8,128)(2,1)S(1)}, bf16[2,128,512]{2,1,0:T(8,128)(2,1)S(1)}, u32[]{:S(2)}, u32[]{:S(2)}) collective-permute-start(bf16[2,128,512]{2,1,0:T(8,128)(2,1)S(1)} %fusion.68), channel_id=1, source_target_pairs={{0,12},{1,13},{2,14},{3,15},{4,0},{5,1},{6,2},{7,3},{8,4},{9,5},{1... | collective-permute-start | bytes 786440 | tf_op jit(solution)/shard_map/ppermute | solution.py:81
  249.1 11.2 %collective-permute-start.2 = (bf16[2,128,512]{2,1,0:T(8,128)(2,1)S(1)}, bf16[2,128,512]{2,1,0:T(8,128)(2,1)S(1)}, u32[]{:S(2)}, u32[]{:S(2)}) collective-permute-start(bf16[2,128,512]{2,1,0:T(8,128)(2,1)S(1)} %fusion.74), channel_id=1, source_target_pairs={{0,4},{1,5},{2,6},{3,7},{4,8},{5,9},{6,10},{7,11},{8,12},{9,13},{1... | collective-permute-start | bytes 786440 | tf_op jit(solution)/shard_map/ppermute | solution.py:80
  249.3 11.1 %collective-permute-start.5 = (bf16[2,128,512]{2,1,0:T(8,128)(2,1)S(1)}, bf16[2,128,512]{2,1,0:T(8,128)(2,1)S(1)}, u32[]{:S(2)}, u32[]{:S(2)}) collective-permute-start(bf16[2,128,512]{2,1,0:T(8,128)(2,1)S(1)} %fusion.72), channel_id=1, source_target_pairs={{0,12},{1,13},{2,14},{3,15},{4,0},{5,1},{6,2},{7,3},{8,4},{9,5},{1... | collective-permute-start | bytes 786440 | tf_op jit(solution)/shard_map/ppermute | solution.py:81
  254.8 11.2 %collective-permute-start.11 = (bf16[2,128,512]{2,1,0:T(8,128)(2,1)S(1)}, bf16[2,128,512]{2,1,0:T(8,128)(2,1)S(1)}, u32[]{:S(2)}, u32[]{:S(2)}) collective-permute-start(bf16[2,128,512]{2,1,0:T(8,128)(2,1)S(1)} %fusion.69), channel_id=1, source_target_pairs={{0,4},{1,5},{2,6},{3,7},{4,8},{5,9},{6,10},{7,11},{8,12},{9,13},{1... | collective-permute-start | bytes 786440 | tf_op jit(solution)/shard_map/ppermute | solution.py:80
  254.9 11.1 %collective-permute-start.14 = (bf16[2,128,512]{2,1,0:T(8,128)(2,1)S(1)}, bf16[2,128,512]{2,1,0:T(8,128)(2,1)S(1)}, u32[]{:S(2)}, u32[]{:S(2)}) collective-permute-start(bf16[2,128,512]{2,1,0:T(8,128)(2,1)S(1)} %fusion.67), channel_id=1, source_target_pairs={{0,12},{1,13},{2,14},{3,15},{4,0},{5,1},{6,2},{7,3},{8,4},{9,5},{1... | collective-permute-start | bytes 786440 | tf_op jit(solution)/shard_map/ppermute | solution.py:81
  260.4 9.8 %collective-permute-start.3 = (bf16[2,128,512]{2,1,0:T(8,128)(2,1)S(1)}, bf16[2,128,512]{2,1,0:T(8,128)(2,1)S(1)}, u32[]{:S(2)}, u32[]{:S(2)}) collective-permute-start(bf16[2,128,512]{2,1,0:T(8,128)(2,1)S(1)} %fusion.73), channel_id=1, source_target_pairs={{0,4},{1,5},{2,6},{3,7},{4,8},{5,9},{6,10},{7,11},{8,12},{9,13},{1... | collective-permute-start | bytes 786440 | tf_op jit(solution)/shard_map/ppermute | solution.py:80
  260.5 12.0 %copy-start.4 = (bf16[2048,128]{1,0:T(8,128)(2,1)S(1)}, bf16[2048,128]{1,0:T(8,128)(2,1)}, u32[]{:S(2)}) copy-start(bf16[2048,128]{1,0:T(8,128)(2,1)} %get-tuple-element.114) | copy-start | bytes 1572868
  260.6 12.0 %copy-start.5 = (bf16[2048,128]{1,0:T(8,128)(2,1)S(1)}, bf16[2048,128]{1,0:T(8,128)(2,1)}, u32[]{:S(2)}) copy-start(bf16[2048,128]{1,0:T(8,128)(2,1)} %get-tuple-element.117) | copy-start | bytes 1572868
  260.6 9.7 %collective-permute-start.6 = (bf16[2,128,512]{2,1,0:T(8,128)(2,1)S(1)}, bf16[2,128,512]{2,1,0:T(8,128)(2,1)S(1)}, u32[]{:S(2)}, u32[]{:S(2)}) collective-permute-start(bf16[2,128,512]{2,1,0:T(8,128)(2,1)S(1)} %fusion.71), channel_id=1, source_target_pairs={{0,12},{1,13},{2,14},{3,15},{4,0},{5,1},{6,2},{7,3},{8,4},{9,5},{1... | collective-permute-start | bytes 786440 | tf_op jit(solution)/shard_map/ppermute | solution.py:81
  266.1 12.1 %collective-permute-start.15 = (bf16[128,1024]{1,0:T(8,128)(2,1)S(1)}, bf16[128,1024]{1,0:T(8,128)(2,1)}, u32[]{:S(2)}, u32[]{:S(2)}) collective-permute-start(bf16[128,1024]{1,0:T(8,128)(2,1)S(1)} %fusion.86), channel_id=1, source_target_pairs={{0,2},{1,3},{2,0},{3,1},{4,6},{5,7},{6,4},{7,5},{8,10},{9,11},{10,... | collective-permute-start | bytes 786440 | tf_op jit(solution)/shard_map/ppermute | solution.py:96
  271.1 8.1 %collective-permute-start.7 = (bf16[128,1024]{1,0:T(8,128)(2,1)}, bf16[128,1024]{1,0:T(8,128)(2,1)}, u32[]{:S(2)}, u32[]{:S(2)}) collective-permute-start(bf16[128,1024]{1,0:T(8,128)(2,1)} %fusion.85), channel_id=1, source_target_pairs={{0,2},{1,3},{2,0},{3,1},{4,6},{5,7},{6,4},{7,5},{8,10},{9,11},{10,... | collective-permute-start | bytes 786440 | tf_op jit(solution)/shard_map/ppermute | solution.py:96
  (7 other events, 20.1 us)
Sparse Core Ops, SparseCore 0:
  10.6 54.5 all-gather.3
  66.9 58.6 all-gather.5
  132.4 52.2 all-gather.7
where the time goes:
time: 288 us
  waiting for transfers between devices  118 us (41%)
  matrix products  66 us (23%)
  starting transfers between devices  23.9 us (8%)
  other arithmetic  23 us (8%)
  blocking collectives  20.5 us (7%)
  local copies, waits for them, and re-layouts  15.6 us (5%)
  between operations  14.4 us (5%)
  loops' own time  6.69 us (2%)
    all_gather x1, waiting for transfers between devices, shards(): lax.all_gather(rms_scale(tokens, attention_gain), 'tensor', axis=0, tiled...  52.3 us
    all_gather x1, waiting for transfers between devices, shards(): normed_stream = lax.all_gather(normed_ffn, 'tensor', axis=0, tiled=True)  52 us
    all_to_all x1, blocking collectives, shards(): lax.all_to_all(context.reshape(groups, tok_dev, inner), 'tensor', split_a...  20.5 us
    ppermute x6, starting transfers between devices, ring_reduce_scatter(): recv_b = lax.ppermute(carry_b, 'tensor', backward_pairs)  17.7 us
    dot_general x4, matrix products, shards(): jnp.dot(rows, projection, preferred_element_type=jnp.float32)  14.6 us
    ppermute x6, waiting for transfers between devices, ring_reduce_scatter(): recv_f = lax.ppermute(carry_f, 'tensor', forward_pairs)  12.5 us
    dot_general x1, matrix products, shards(): jnp.dot(picked, expert_gate[local], preferred_element_type=jnp.float32)  9.35 us
    dot_general x2, matrix products, shards(): jnp.dot(expert_hidden[local], expert_down[local][:, columns], preferred_e...  7.49 us
  transfers between devices with their start and end apart: 19, of which 7 were waited for; matrix products, arithmetic and copies ran while one was open for 19% of the time, Pallas kernels for 0%

commit v1 on v0

--- a/solution.py
+++ b/solution.py
@@ -143,7 +143,9 @@
     normed_ffn = rms_scale(residual, ffn_gain)
     pieces = 2
     piece_width = model_width // pieces
-    normed_stream = lax.all_gather(normed_ffn, "tensor", axis=0, tiled=True)
+    normed_stream = jnp.concatenate(
+        lax.all_to_all(jnp.stack([normed_ffn] * lax.axis_size("tensor")), "tensor", 0, 0), axis=0
+    )
     local_experts = expert_gate.shape[0]
     expert_count = local_experts * groups
     capacity = tok_dev * TOP // expert_count + tok_dev // 8

time: 288 us -> 341 us (1.18)
  waiting for transfers between devices: 118 us -> 161 us
  local copies, waits for them, and re-layouts: 15.6 us -> 20.1 us
  starting transfers between devices: 23.9 us -> 27.4 us
    all_to_all x0 -> x1, waiting for transfers between devices: none -> 94.7 us  [shards(): lax.all_to_all(jnp.stack([normed_ffn] * lax.axis_size('tensor')), 'tensor...]
    all_gather x1 -> x0, waiting for transfers between devices: 52 us -> none  [shards(): normed_stream = lax.all_gather(normed_ffn, 'tensor', axis=0, tiled=True)]
    all_to_all x0 -> x1, starting transfers between devices: none -> 5.07 us  [shards(): lax.all_to_all(jnp.stack([normed_ffn] * lax.axis_size('tensor')), 'tensor...]
    another operation x0 -> x1, local copies, waits for them, and re-layouts: none -> 4.3 us  [shards(): jnp.stack([normed_ffn] * lax.axis_size('tensor'))]
  transfers between devices with their start and end apart: 19 -> 19, of which waited for: 7 -> 7; matrix products, arithmetic and copies ran while one was open for 19% -> 16% of each run, Pallas kernels for 0% -> 0%
where the time goes in v1:
time: 341 us
  waiting for transfers between devices  161 us (47%)
  matrix products  68.5 us (20%)
  starting transfers between devices  27.4 us (8%)
  other arithmetic  22.5 us (7%)
  local copies, waits for them, and re-layouts  20.1 us (6%)
  blocking collectives  18.8 us (6%)
  between operations  14.7 us (4%)
  loops' own time  7.77 us (2%)
    all_to_all x1, waiting for transfers between devices, shards(): lax.all_to_all(jnp.stack([normed_ffn] * lax.axis_size('tensor')), 'tensor...  94.7 us
    all_gather x1, waiting for transfers between devices, shards(): lax.all_gather(rms_scale(tokens, attention_gain), 'tensor', axis=0, tiled...  52.4 us
    ppermute x6, starting transfers between devices, ring_reduce_scatter(): recv_b = lax.ppermute(carry_b, 'tensor', backward_pairs)  19.4 us
    all_to_all x1, blocking collectives, shards(): lax.all_to_all(context.reshape(groups, tok_dev, inner), 'tensor', split_a...  18.8 us
    dot_general x4, matrix products, shards(): jnp.dot(rows, projection, preferred_element_type=jnp.float32)  14.7 us
    ppermute x6, waiting for transfers between devices, ring_reduce_scatter(): recv_f = lax.ppermute(carry_f, 'tensor', forward_pairs)  13 us
    dot_general x1, matrix products, shards(): jnp.dot(picked, expert_gate[local], preferred_element_type=jnp.float32)  9.37 us
    another operation x1, loops' own time, attend(): context = lax.map(one_block, starts).reshape(total_tokens, inner)  7.76 us
  transfers between devices with their start and end apart: 19, of which 7 were waited for; matrix products, arithmetic and copies ran while one was open for 16% of the time, Pallas kernels for 0%

profile of v1, /device:TPU:0, one launch (start us, length us, event | category | flops | bytes accessed | tf_op | source)
XLA Modules:
  0.0 340.6 jit_solution(13345252364971754919)
XLA Ops:
  12.9 52.4 %all-gather.3.cloned.1.call-done = bf16[2048,2048]{1,0:T(8,128)(2,1)} async-done(((bf16[128,2048]{1,0:T(8,128)(2,1)}), bf16[2048,2048]{1,0:T(8,128)(2,1)}) %all-gather.3.cloned.1.call-update) | async-done | bytes 8388624 | tf_op jit(solution)/shard_map/all_gather | solution.py:126
  65.2 14.7 %while.21 = (s32[]{:T(128)}, bf16[4,512,384]{2,1,0:T(8,128)(2,1)}, bf16[4,512,2048]{2,1,0:T(8,128)(2,1)}, bf16[2048,384]{1,0:T(8,128)(2,1)S(1)}, s32[]{:T(128)}) while((s32[]{:T(128)}, bf16[4,512,384]{2,1,0:T(8,128)(2,1)}, bf16[4,512,2048]{2,1,0:T(8,128)(2,1)}, bf16[2048,384]{1,0:T(8,128)(2,1)S(1)}, s32[]{:T(128)}) %tuple.60), condition=%wide.region_2.3_spmd, body=%wide.region_1.2_spmd.sunk | while | flops 805502976 | bytes 4064325 | solution.py:128
  65.2 3.6 %fusion.120 = bf16[4,512,384]{2,1,0:T(8,128)(2,1)} fusion(bf16[4,512,384]{2,1,0:T(8,128)(2,1)} %get-tuple-element.199, s32[]{:T(128)S(6)} %copy.34, bf16[2048,384]{1,0:T(8,128)(2,1)S(1)} %get-tuple-element.206, bf16[4,512,2048]{2,1,0:T(8,128)(2,1)} %get-tuple-element.205), kind=kOutput, calls=%fused_computation.7.clone.1 | convolution fusion | flops 805502976 | bytes 4064256 | tf_op jit(solution)/shard_map/while/body/eval_jaxpr/dot_general | solution.py:129
  68.8 3.6 %fusion.120 = bf16[4,512,384]{2,1,0:T(8,128)(2,1)} fusion(bf16[4,512,384]{2,1,0:T(8,128)(2,1)} %get-tuple-element.199, s32[]{:T(128)S(6)} %copy.34, bf16[2048,384]{1,0:T(8,128)(2,1)S(1)} %get-tuple-element.206, bf16[4,512,2048]{2,1,0:T(8,128)(2,1)} %get-tuple-element.205), kind=kOutput, calls=%fused_computation.7.clone.1 | convolution fusion | flops 805502976 | bytes 4064256 | tf_op jit(solution)/shard_map/while/body/eval_jaxpr/dot_general | solution.py:129
  72.4 3.6 %fusion.120 = bf16[4,512,384]{2,1,0:T(8,128)(2,1)} fusion(bf16[4,512,384]{2,1,0:T(8,128)(2,1)} %get-tuple-element.199, s32[]{:T(128)S(6)} %copy.34, bf16[2048,384]{1,0:T(8,128)(2,1)S(1)} %get-tuple-element.206, bf16[4,512,2048]{2,1,0:T(8,128)(2,1)} %get-tuple-element.205), kind=kOutput, calls=%fused_computation.7.clone.1 | convolution fusion | flops 805502976 | bytes 4064256 | tf_op jit(solution)/shard_map/while/body/eval_jaxpr/dot_general | solution.py:129
  76.0 3.9 %fusion.120 = bf16[4,512,384]{2,1,0:T(8,128)(2,1)} fusion(bf16[4,512,384]{2,1,0:T(8,128)(2,1)} %get-tuple-element.199, s32[]{:T(128)S(6)} %copy.34, bf16[2048,384]{1,0:T(8,128)(2,1)S(1)} %get-tuple-element.206, bf16[4,512,2048]{2,1,0:T(8,128)(2,1)} %get-tuple-element.205), kind=kOutput, calls=%fused_computation.7.clone.1 | convolution fusion | flops 805502976 | bytes 4064256 | tf_op jit(solution)/shard_map/while/body/eval_jaxpr/dot_general | solution.py:129
  79.9 2.6 fusion.97
  82.5 24.7 %while.22 = (s32[]{:T(128)}, bf16[4,512,1,128]{3,1,2,0:T(8,128)(2,1)S(1)}, s32[4]{0:T(128)S(1)}, s32[2048]{0:T(1024)S(1)}, bf16[2048,1,128]{2,0,1:T(8,128)(2,1)S...) while((s32[]{:T(128)}, ...), condition=%wide.region_6.7_spmd.clone, body=%wide.region_3.6_spmd.clone.sunk | while | flops 548470272 | bytes 13922475 | solution.py:45
  107.3 18.8 %all_to_all.10 = bf16[16,128,128]{2,1,0:T(8,128)(2,1)S(1)} all-to-all(bf16[16,128,128]{2,1,0:T(8,128)(2,1)S(1)} %bitcast.197), channel_id=1, replica_groups=mesh['dp'=8,'tensor'=16] {'tensor'}, dimensions={0} | all-to-all | bytes 1048576 | tf_op jit(solution)/shard_map/all_to_all | solution.py:137
  126.4 4.7 %multiply_reduce_fusion = (f32[128]{0:T(128)S(1)}, f32[128,2048]{1,0:T(8,128)S(1)}) fusion(bf16[128,2048]{0,1:T(8,128)(2,1)S(1)} %bitcast.190, bf16[2048,2048]{1,0:T(8,128)(2,1)} %all-gather.5.cloned.1.call-done, bf16[128,2048]{1,0:T(8,128)(2,1)S(1)} %copy-done), kind=kOutput, calls=%fused_computation.76 | convolution fusion | flops 1075314560 | bytes 10486272 | tf_op jit(solution)/shard_map/dot_general | solution.py:141
  131.3 4.3 %stack.8 = bf16[16,128,2048]{2,1,0:T(8,128)(2,1)} broadcast(bf16[128,2048]{1,0:T(8,128)(2,1)S(1)} %multiply_convert_fusion.1), dimensions={1,2} | broadcast | bytes 8912896 | tf_op jit(solution)/shard_map/stack | solution.py:147
  135.6 5.1 %all-to-all-start.1 = ((bf16[16,128,2048]{2,1,0:T(8,128)(2,1)}), bf16[16,128,2048]{2,1,0:T(8,128)(2,1)}, u32[]{:S(2)}, u32[]{:S(2)}) async-start(bf16[16,128,2048]{2,1,0:T(8,128)(2,1)} %stack.8), calls=%async_computation.1 | async-start | bytes 16777216 | tf_op jit(solution)/shard_map/all_to_all | solution.py:147
  141.1 94.7 %all-to-all-done.1 = bf16[16,128,2048]{2,1,0:T(8,128)(2,1)} async-done(((bf16[16,128,2048]{2,1,0:T(8,128)(2,1)}), bf16[16,128,2048]{2,1,0:T(8,128)(2,1)}, u32[]{:S(2)}, u32[]{:S(2)}) %all-to-all-start.1) | async-done | bytes 8388640 | tf_op jit(solution)/shard_map/all_to_all | solution.py:147
  235.9 4.8 %convolution_convert_fusion = bf16[16,64,2048]{2,1,0:T(8,128)(2,1)S(1)} fusion(bf16[16,128,2048]{2,1,0:T(8,128)(2,1)} %all-to-all-done.1, s32[16,128]{1,0:T(8,128)S(1)} %bitcast_subtract_fusion, pred[16,128]{1,0:T(8,128)(4,1)S(1)} %broadcast_compare_fusion.1), kind=kOutput, calls=%fused_computation.38 | convolution fusion | flops 539230208 | bytes 12593152 | tf_op jit(solution)/shard_map/bst,btd->bsd/dot_general | solution.py:176
  240.7 9.4 %fusion.32 = f32[1024,1408]{1,0:T(8,128)S(1)} fusion(bf16[1024,2048]{1,0:T(8,128)(2,1)S(1)} %bitcast.182, bf16[1,2048,1408]{2,1,0:T(8,128)(2,1)} %param.32), kind=kOutput, calls=%fused_computation.33 | convolution fusion | flops 5905580032 | bytes 15728640 | tf_op jit(solution)/shard_map/dot_general | solution.py:183
  250.1 7.1 %multiply_convert_fusion = bf16[1024,1408]{1,0:T(8,128)(2,1)S(1)} fusion(f32[1024,1408]{1,0:T(8,128)S(1)} %fusion.32, bf16[1024,2048]{1,0:T(8,128)(2,1)S(1)} %bitcast.183, bf16[1,2048,1408]{2,1,0:T(8,128)(2,1)S(1)} %bitcast.201), kind=kOutput, calls=%fused_computation.35 | convolution fusion | flops 5914230784 | bytes 18612224 | tf_op jit(solution)/shard_map/dot_general | solution.py:186
  257.2 3.6 %fusion.45 = bf16[1024,1024]{1,0:T(8,128)(2,1)S(1)} fusion(bf16[1024,1408]{1,0:T(8,128)(2,1)S(1)} %multiply_convert_fusion, bf16[1408,2048]{1,0:T(8,128)(2,1)S(1)} %bitcast.204), kind=kOutput, calls=%fused_computation.51 | convolution fusion | flops 2953838592 | bytes 7864320 | tf_op jit(solution)/shard_map/dot_general | solution.py:200
  260.9 3.6 %fusion.42 = bf16[1024,1024]{1,0:T(8,128)(2,1)S(1)} fusion(bf16[1024,1408]{1,0:T(8,128)(2,1)S(1)} %multiply_convert_fusion, bf16[1408,2048]{1,0:T(8,128)(2,1)S(1)} %bitcast.205), kind=kOutput, calls=%fused_computation.50 | convolution fusion | flops 2953838592 | bytes 7864320 | tf_op jit(solution)/shard_map/dot_general | solution.py:200
  264.5 5.8 %fusion.49 = f32[2048,352]{0,1:T(8,128)S(1)} fusion(bf16[2048,2048]{1,0:T(8,128)(2,1)} %bitcast.10, bf16[2048,176]{0,1:T(8,128)(2,1)S(1)} %copy-done.10, bf16[2048,176]{0,1:T(8,128)(2,1)S(1)} %copy-done.11), kind=kOutput, calls=%fused_computation.57 | convolution fusion | flops 2955673600 | bytes 12713984 | tf_op jit(solution)/shard_map/dot_general | solution.py:170
  281.4 3.2 convert_add_fusion
  285.6 3.0 collective-permute-start.12
  288.7 2.5 convert_add_fusion.1
  292.0 3.2 collective-permute-start.4
  295.5 3.3 collective-permute-start.13
  298.7 3.7 %collective-permute-done.1 = bf16[2,128,512]{2,1,0:T(8,128)(2,1)S(1)} collective-permute-done((bf16[2,128,512]{2,1,0:T(8,128)(2,1)S(1)}, bf16[2,128,512]{2,1,0:T(8,128)(2,1)S(1)}, u32[]{:S(2)}, u32[]{:S(2)}) %collective-permute-start.1) | collective-permute-done | bytes 262176 | tf_op jit(solution)/shard_map/ppermute | solution.py:80
  302.7 3.3 collective-permute-start.5
  305.9 2.1 collective-permute-done.10
  308.5 3.3 collective-permute-start.14
  313.9 3.3 collective-permute-start.6
  317.2 2.1 collective-permute-done.11
  320.2 3.3 collective-permute-done.3
  327.4 3.4 scatter_fusion
  (137 shorter events, 46.9 us)
Async XLA Ops:
  7.2 58.1 %all-gather.3.cloned.1.call-start = ((), (), s32[]{:S(2)}) async-start(), calls=%async_computation.2 | async-start | bytes 8912896 | tf_op jit(solution)/shard_map/all_gather | solution.py:126
  10.5 115.9 %all-gather.5.cloned.1.call-start = ((), (), s32[]{:S(2)}) async-start(), calls=%async_computation.3 | async-start | bytes 8912896 | tf_op jit(solution)/shard_map/all_gather | solution.py:127
  82.5 43.9 %copy-start = (bf16[128,2048]{1,0:T(8,128)(2,1)S(1)}, bf16[128,2048]{1,0:T(8,128)(2,1)}, u32[]{:S(2)}) copy-start(bf16[128,2048]{1,0:T(8,128)(2,1)} %param.21) | copy-start | bytes 1572868
  126.4 4.8 %copy-start.9 = (f32[2048]{0:T(1024)S(1)}, f32[2048]{0:T(1024)}, u32[]{:S(2)}) copy-start(f32[2048]{0:T(1024)} %param.28) | copy-start | bytes 24580
  135.6 5.1 %copy-start.6 = (f32[2048,6]{0,1:T(8,128)S(1)}, f32[2048,6]{0,1:T(8,128)}, u32[]{:S(2)}) copy-start(f32[2048,6]{0,1:T(8,128)} %param.36) | copy-start | bytes 147460
  135.6 5.1 %copy-start.7 = (s32[2048,6]{0,1:T(8,128)S(1)}, s32[2048,6]{0,1:T(8,128)}, u32[]{:S(2)}) copy-start(s32[2048,6]{0,1:T(8,128)} %param.35) | copy-start | bytes 147460
  135.6 100.2 %all-to-all-start.1 = ((bf16[16,128,2048]{2,1,0:T(8,128)(2,1)}), bf16[16,128,2048]{2,1,0:T(8,128)(2,1)}, u32[]{:S(2)}, u32[]{:S(2)}) async-start(bf16[16,128,2048]{2,1,0:T(8,128)(2,1)} %stack.8), calls=%async_computation.1 | async-start | bytes 16777216 | tf_op jit(solution)/shard_map/all_to_all | solution.py:147
  235.9 14.2 %slice-start = ((s8[5767168]{0:T(1024)(128)(4,1)}), s8[4194304]{0:T(1024)(128)(4,1)S(1)}, s32[]{:S(2)}) async-start(s8[5767168]{0:T(1024)(128)(4,1)} %bitcast.200), calls=%async_computation.4 | async-start | bytes 8388608
  240.6 9.4 %slice-start.1 = ((s8[5767168]{0:T(1024)(128)(4,1)}), s8[1572864]{0:T(1024)(128)(4,1)S(1)}, s32[]{:S(2)}) async-start(s8[5767168]{0:T(1024)(128)(4,1)} %bitcast.200), calls=%async_computation.5 | async-start | bytes 3145728
  240.7 16.5 %slice-start.2 = ((s8[5767168]{0:T(1024)(128)(4,1)}), s8[4194304]{0:T(1024)(128)(4,1)S(1)}, s32[]{:S(2)}) async-start(s8[5767168]{0:T(1024)(128)(4,1)} %bitcast.202), calls=%async_computation.6 | async-start | bytes 8388608
  250.1 7.1 %slice-start.3 = ((s8[5767168]{0:T(1024)(128)(4,1)}), s8[1572864]{0:T(1024)(128)(4,1)S(1)}, s32[]{:S(2)}) async-start(s8[5767168]{0:T(1024)(128)(4,1)} %bitcast.202), calls=%async_computation.7 | async-start | bytes 3145728
  260.8 3.7 %copy-start.10 = (bf16[2048,176]{0,1:T(8,128)(2,1)S(1)}, bf16[2048,176]{0,1:T(8,128)(2,1)}, u32[]{:S(2)}) copy-start(bf16[2048,176]{0,1:T(8,128)(2,1)} %param.30) | copy-start | bytes 2162692
  260.9 3.7 %copy-start.11 = (bf16[2048,176]{0,1:T(8,128)(2,1)S(1)}, bf16[2048,176]{0,1:T(8,128)(2,1)}, u32[]{:S(2)}) copy-start(bf16[2048,176]{0,1:T(8,128)(2,1)} %param.29) | copy-start | bytes 2162692
  275.6 5.8 %collective-permute-start.8 = (bf16[4,2,128,1024]{3,2,1,0:T(8,128)(2,1)}, bf16[4,2,128,1024]{3,2,1,0:T(8,128)(2,1)}, u32[]{:S(2)}, u32[]{:S(2)}) collective-permute-start(bf16[4,2,128,1024]{3,2,1,0:T(8,128)(2,1)} %dynamic-slice_bitcast_fusion), channel_id=1, source_target_pairs={{0,1},{1,0},{2,3},{3,2},{4,5},{5,4},{6,7},{7,6},{8,9},{9,8},{10,11... | collective-permute-start | bytes 6291464 | tf_op jit(solution)/shard_map/ppermute | solution.py:68
  280.8 7.9 %collective-permute-start = (bf16[4,2,128,1024]{3,2,1,0:T(8,128)(2,1)S(1)}, bf16[4,2,128,1024]{3,2,1,0:T(8,128)(2,1)}, u32[]{:S(2)}, u32[]{:S(2)}) collective-permute-start(bf16[4,2,128,1024]{3,2,1,0:T(8,128)(2,1)S(1)} %dynamic-slice_bitcast_fusion.1), channel_id=1, source_target_pairs={{0,1},{1,0},{2,3},{3,2},{4,5},{5,4},{6,7},{7,6},{8,9},{9,8},{10,11... | collective-permute-start | bytes 6291464 | tf_op jit(solution)/shard_map/ppermute | solution.py:68
  284.6 4.1 %copy-start.2 = (bf16[2048,1024]{1,0:T(8,128)(2,1)S(1)}, bf16[2048,1024]{1,0:T(8,128)(2,1)}, u32[]{:S(2)}) copy-start(bf16[2048,1024]{1,0:T(8,128)(2,1)} %copy-done.1) | copy-start | bytes 12582916
  285.3 10.0 %collective-permute-start.9 = (bf16[2,128,512]{2,1,0:T(8,128)(2,1)S(1)}, bf16[2,128,512]{2,1,0:T(8,128)(2,1)S(1)}, u32[]{:S(2)}, u32[]{:S(2)}) collective-permute-start(bf16[2,128,512]{2,1,0:T(8,128)(2,1)S(1)} %fusion.83), channel_id=1, source_target_pairs={{0,4},{1,5},{2,6},{3,7},{4,8},{5,9},{6,10},{7,11},{8,12},{9,13},{1... | collective-permute-start | bytes 786440 | tf_op jit(solution)/shard_map/ppermute | solution.py:80
  285.6 9.7 %collective-permute-start.12 = (bf16[2,128,512]{2,1,0:T(8,128)(2,1)S(1)}, bf16[2,128,512]{2,1,0:T(8,128)(2,1)S(1)}, u32[]{:S(2)}, u32[]{:S(2)}) collective-permute-start(bf16[2,128,512]{2,1,0:T(8,128)(2,1)S(1)} %fusion.84), channel_id=1, source_target_pairs={{0,12},{1,13},{2,14},{3,15},{4,0},{5,1},{6,2},{7,3},{8,4},{9,5},{1... | collective-permute-start | bytes 786440 | tf_op jit(solution)/shard_map/ppermute | solution.py:81
  291.9 10.5 %collective-permute-start.1 = (bf16[2,128,512]{2,1,0:T(8,128)(2,1)S(1)}, bf16[2,128,512]{2,1,0:T(8,128)(2,1)S(1)}, u32[]{:S(2)}, u32[]{:S(2)}) collective-permute-start(bf16[2,128,512]{2,1,0:T(8,128)(2,1)S(1)} %fusion.81), channel_id=1, source_target_pairs={{0,4},{1,5},{2,6},{3,7},{4,8},{5,9},{6,10},{7,11},{8,12},{9,13},{1... | collective-permute-start | bytes 786440 | tf_op jit(solution)/shard_map/ppermute | solution.py:80
  292.0 10.6 %collective-permute-start.4 = (bf16[2,128,512]{2,1,0:T(8,128)(2,1)S(1)}, bf16[2,128,512]{2,1,0:T(8,128)(2,1)S(1)}, u32[]{:S(2)}, u32[]{:S(2)}) collective-permute-start(bf16[2,128,512]{2,1,0:T(8,128)(2,1)S(1)} %fusion.82), channel_id=1, source_target_pairs={{0,12},{1,13},{2,14},{3,15},{4,0},{5,1},{6,2},{7,3},{8,4},{9,5},{1... | collective-permute-start | bytes 786440 | tf_op jit(solution)/shard_map/ppermute | solution.py:81
  295.3 12.7 %collective-permute-start.10 = (bf16[2,128,512]{2,1,0:T(8,128)(2,1)S(1)}, bf16[2,128,512]{2,1,0:T(8,128)(2,1)S(1)}, u32[]{:S(2)}, u32[]{:S(2)}) collective-permute-start(bf16[2,128,512]{2,1,0:T(8,128)(2,1)S(1)} %fusion.70), channel_id=1, source_target_pairs={{0,4},{1,5},{2,6},{3,7},{4,8},{5,9},{6,10},{7,11},{8,12},{9,13},{1... | collective-permute-start | bytes 786440 | tf_op jit(solution)/shard_map/ppermute | solution.py:80
  295.5 13.0 %collective-permute-start.13 = (bf16[2,128,512]{2,1,0:T(8,128)(2,1)S(1)}, bf16[2,128,512]{2,1,0:T(8,128)(2,1)S(1)}, u32[]{:S(2)}, u32[]{:S(2)}) collective-permute-start(bf16[2,128,512]{2,1,0:T(8,128)(2,1)S(1)} %fusion.68), channel_id=1, source_target_pairs={{0,12},{1,13},{2,14},{3,15},{4,0},{5,1},{6,2},{7,3},{8,4},{9,5},{1... | collective-permute-start | bytes 786440 | tf_op jit(solution)/shard_map/ppermute | solution.py:81
  302.5 11.2 %collective-permute-start.2 = (bf16[2,128,512]{2,1,0:T(8,128)(2,1)S(1)}, bf16[2,128,512]{2,1,0:T(8,128)(2,1)S(1)}, u32[]{:S(2)}, u32[]{:S(2)}) collective-permute-start(bf16[2,128,512]{2,1,0:T(8,128)(2,1)S(1)} %fusion.74), channel_id=1, source_target_pairs={{0,4},{1,5},{2,6},{3,7},{4,8},{5,9},{6,10},{7,11},{8,12},{9,13},{1... | collective-permute-start | bytes 786440 | tf_op jit(solution)/shard_map/ppermute | solution.py:80
  302.7 11.1 %collective-permute-start.5 = (bf16[2,128,512]{2,1,0:T(8,128)(2,1)S(1)}, bf16[2,128,512]{2,1,0:T(8,128)(2,1)S(1)}, u32[]{:S(2)}, u32[]{:S(2)}) collective-permute-start(bf16[2,128,512]{2,1,0:T(8,128)(2,1)S(1)} %fusion.72), channel_id=1, source_target_pairs={{0,12},{1,13},{2,14},{3,15},{4,0},{5,1},{6,2},{7,3},{8,4},{9,5},{1... | collective-permute-start | bytes 786440 | tf_op jit(solution)/shard_map/ppermute | solution.py:81
  308.1 11.2 %collective-permute-start.11 = (bf16[2,128,512]{2,1,0:T(8,128)(2,1)S(1)}, bf16[2,128,512]{2,1,0:T(8,128)(2,1)S(1)}, u32[]{:S(2)}, u32[]{:S(2)}) collective-permute-start(bf16[2,128,512]{2,1,0:T(8,128)(2,1)S(1)} %fusion.69), channel_id=1, source_target_pairs={{0,4},{1,5},{2,6},{3,7},{4,8},{5,9},{6,10},{7,11},{8,12},{9,13},{1... | collective-permute-start | bytes 786440 | tf_op jit(solution)/shard_map/ppermute | solution.py:80
  308.5 10.8 %collective-permute-start.14 = (bf16[2,128,512]{2,1,0:T(8,128)(2,1)S(1)}, bf16[2,128,512]{2,1,0:T(8,128)(2,1)S(1)}, u32[]{:S(2)}, u32[]{:S(2)}) collective-permute-start(bf16[2,128,512]{2,1,0:T(8,128)(2,1)S(1)} %fusion.67), channel_id=1, source_target_pairs={{0,12},{1,13},{2,14},{3,15},{4,0},{5,1},{6,2},{7,3},{8,4},{9,5},{1... | collective-permute-start | bytes 786440 | tf_op jit(solution)/shard_map/ppermute | solution.py:81
  313.7 9.8 %collective-permute-start.3 = (bf16[2,128,512]{2,1,0:T(8,128)(2,1)S(1)}, bf16[2,128,512]{2,1,0:T(8,128)(2,1)S(1)}, u32[]{:S(2)}, u32[]{:S(2)}) collective-permute-start(bf16[2,128,512]{2,1,0:T(8,128)(2,1)S(1)} %fusion.73), channel_id=1, source_target_pairs={{0,4},{1,5},{2,6},{3,7},{4,8},{5,9},{6,10},{7,11},{8,12},{9,13},{1... | collective-permute-start | bytes 786440 | tf_op jit(solution)/shard_map/ppermute | solution.py:80
  313.9 11.2 %copy-start.4 = (bf16[2048,128]{1,0:T(8,128)(2,1)S(1)}, bf16[2048,128]{1,0:T(8,128)(2,1)}, u32[]{:S(2)}) copy-start(bf16[2048,128]{1,0:T(8,128)(2,1)} %get-tuple-element.114) | copy-start | bytes 1572868
  313.9 11.2 %copy-start.5 = (bf16[2048,128]{1,0:T(8,128)(2,1)S(1)}, bf16[2048,128]{1,0:T(8,128)(2,1)}, u32[]{:S(2)}) copy-start(bf16[2048,128]{1,0:T(8,128)(2,1)} %get-tuple-element.117) | copy-start | bytes 1572868
  313.9 9.7 %collective-permute-start.6 = (bf16[2,128,512]{2,1,0:T(8,128)(2,1)S(1)}, bf16[2,128,512]{2,1,0:T(8,128)(2,1)S(1)}, u32[]{:S(2)}, u32[]{:S(2)}) collective-permute-start(bf16[2,128,512]{2,1,0:T(8,128)(2,1)S(1)} %fusion.71), channel_id=1, source_target_pairs={{0,12},{1,13},{2,14},{3,15},{4,0},{5,1},{6,2},{7,3},{8,4},{9,5},{1... | collective-permute-start | bytes 786440 | tf_op jit(solution)/shard_map/ppermute | solution.py:81
  319.5 11.3 %collective-permute-start.15 = (bf16[128,1024]{1,0:T(8,128)(2,1)S(1)}, bf16[128,1024]{1,0:T(8,128)(2,1)}, u32[]{:S(2)}, u32[]{:S(2)}) collective-permute-start(bf16[128,1024]{1,0:T(8,128)(2,1)S(1)} %fusion.86), channel_id=1, source_target_pairs={{0,2},{1,3},{2,0},{3,1},{4,6},{5,7},{6,4},{7,5},{8,10},{9,11},{10,... | collective-permute-start | bytes 786440 | tf_op jit(solution)/shard_map/ppermute | solution.py:96
  324.4 7.3 %collective-permute-start.7 = (bf16[128,1024]{1,0:T(8,128)(2,1)}, bf16[128,1024]{1,0:T(8,128)(2,1)}, u32[]{:S(2)}, u32[]{:S(2)}) collective-permute-start(bf16[128,1024]{1,0:T(8,128)(2,1)} %fusion.85), channel_id=1, source_target_pairs={{0,2},{1,3},{2,0},{3,1},{4,6},{5,7},{6,4},{7,5},{8,10},{9,11},{10,... | collective-permute-start | bytes 786440 | tf_op jit(solution)/shard_map/ppermute | solution.py:96
  (5 other events, 12.3 us)
Sparse Core Ops, SparseCore 0:
  10.6 54.5 all-gather.2
  66.9 58.6 all-gather.4
